TPU v7x, 256 devices: a whole 4x4x8 slice. The times are simulated.
256 devices in a mesh: role: 2 (over core), dp: 16 (over x, y), tensor: 8 (over z).
Axes of the slice: x: 4, y: 4, z: 8, core: 2. Of those that a mesh axis runs over, the one named last changes fastest.
Arguments:
- queries: bfloat16 [1024, 128, 576], P(('dp', 'tensor'), 'role'), may hold values from -13 to 13
- latent_cache: bfloat16 [512, 1024, 576], P(('dp', 'tensor')), may hold values from -4 to 4
- new_latent: bfloat16 [1024, 576], P(('dp', 'tensor')), may hold values from -9 to 9
- cache_lengths: int32 [512], P(('dp', 'tensor')), may hold values from 2 to 1024
- value_proj: bfloat16 [128, 512, 128], P(('role', 'tensor')), may hold values from -1 to 1
- out_proj: bfloat16 [16384, 7168], P(('role', 'tensor'), 'dp'), may hold values from -0.046875 to 0.046875
- residual: bfloat16 [1024, 7168], P(('role', 'tensor'), 'dp'), may hold values from -68 to 68
- norm_gain: bfloat16 [7168], replicated, may hold values from 0.5 to 1.5
- routes: int32 [1024, 8], P(('role', 'tensor')), may hold values from 0 to 15, all different within a row; in each aligned block of 64 rows (0 to 63, 64 to 127, ...) at most 40 rows name the same one
- gate_values: float32 [1024, 8], P(('role', 'tensor')), may hold values from 0.2 to 0.8
- tenant_ids: int32 [1024], P(('role', 'tensor')), may hold values from 0 to 2
- expert_gate_weight: bfloat16 [16, 7168, 2048], P('dp', None, ('role', 'tensor')), may hold values from -0.0625 to 0.0625
- expert_up_weight: bfloat16 [16, 7168, 2048], P('dp', None, ('role', 'tensor')), may hold values from -0.0625 to 0.0625
- expert_down_weight: bfloat16 [16, 2048, 7168], P('dp', ('role', 'tensor')), may hold values from -0.125 to 0.125
- left_delta_factor: bfloat16 [3, 16, 2048, 64], P(None, 'dp', ('role', 'tensor')), may hold values from -0.125 to 0.125
- factor_right: bfloat16 [3, 16, 64, 7168], P(None, 'dp'), may hold values from -0.75 to 0.75
Outputs:
- mixed: bfloat16 [1024, 7168], P(('role', 'tensor'), 'dp')
Inputs may be any that keep to these rules, and one draw needn't show every extreme that they name: `routes`: in each aligned block of 64 tokens no expert is named by more than 40 of them.
All inputs are finite; a program needn't handle non-finite values.
Results may differ from a plain program's by a relative error of at most 0.008.
Values may be sent and summed in bfloat16 or wider, within the bound.
No kernel may reach another device: no remote copies, remote signals or barrier semaphores. Data moves between devices by JAX's collectives and lax.ppermute only.
A program may use at most 128 MiB of HBM per device.

v0:
```python
import jax
import jax.numpy as jnp
from jax import lax
from jax.sharding import PartitionSpec as P

LAT = 512
EXPERTS = 16
TEN = 3
SCORE_SCALE = 0.07216878364870323
NORM_EPS = 1e-06
MASKED = -1e30
RT = ("role", "tensor")


def rms_rows(input_rows, norm_gain):
    wide = input_rows.astype(jnp.float32)
    scale = lax.rsqrt(jnp.mean(wide * wide, axis=-1, keepdims=True) + NORM_EPS)
    return (wide * scale * norm_gain.astype(jnp.float32)).astype(jnp.bfloat16)


def slot_table(routes, expert, capacity):
    hit = jnp.any(routes == expert, axis=-1).astype(jnp.int32)
    earlier = jnp.cumsum(hit, axis=-1) - hit
    slot_ids = jnp.arange(capacity, dtype=jnp.int32)
    return (hit[..., None, :] > 0) & (earlier[..., None, :] == slot_ids[:, None])


def local(
    queries,
    latent_cache,
    new_latent,
    cache_lengths,
    value_proj,
    out_proj,
    residual,
    norm_gain,
    routes,
    gate_values,
    tenant_ids,
    expert_gate_weight,
    expert_up_weight,
    expert_down_weight,
    left_delta_factor,
    factor_right,
):
    n_slices = lax.axis_size(RT)
    slice_idx = lax.axis_index(RT)
    group_rows = residual.shape[0]
    capacity = 5 * group_rows // 8
    model_width = expert_down_weight.shape[2]
    col_width = model_width // n_slices
    expert = lax.axis_index("dp")
    labels = jnp.arange(EXPERTS, dtype=jnp.int32)
    table = slot_table(routes, labels[:, None, None], capacity)
    mine = lax.dynamic_index_in_dim(table, expert, 0, keepdims=False)
    mine_owner = jnp.sum(mine.astype(jnp.int32) * tenant_ids[None, :], axis=1)
    hidden_slice = expert_down_weight.shape[1]
    down_local = expert_down_weight[0].reshape(hidden_slice, n_slices, col_width)
    down_local = jnp.transpose(down_local, (1, 0, 2))
    left_local = left_delta_factor[:, 0]
    tenants, _, rank = left_local.shape
    left_local = jnp.transpose(left_local, (1, 0, 2)).reshape(1, hidden_slice, tenants * rank)
    left_local = jnp.broadcast_to(left_local, (n_slices, hidden_slice, tenants * rank))
    down_pack = jnp.concatenate([down_local, left_local], axis=2)
    pack_width = down_pack.shape[2]
    info = mine_owner.astype(jnp.bfloat16)
    info_rows = jnp.zeros((8, pack_width), jnp.bfloat16).at[0, : info.shape[0]].set(info)
    info_rows = jnp.broadcast_to(info_rows[None], (n_slices, 8, pack_width))
    down_pack = jnp.concatenate([down_pack, info_rows], axis=1)
    down_pack = lax.all_to_all(down_pack, RT, split_axis=0, concat_axis=0, tiled=True)
    right_w = lax.dynamic_slice_in_dim(factor_right[:, 0], slice_idx * col_width, col_width, 2)
    seq_count, context, width = latent_cache.shape
    local_heads = queries.shape[1]
    paired = queries.reshape(seq_count, 2, local_heads, width)
    scores = (
        jnp.einsum("sqhd,spd->sqhp", paired, latent_cache, preferred_element_type=jnp.float32)
        * SCORE_SCALE
    )
    present = jnp.arange(context, dtype=jnp.int32)[None, :] < cache_lengths[:, None]
    scores = jnp.where(present[:, None, None, :], scores, MASKED)
    fresh_keys = new_latent.reshape(seq_count, 2, width)
    fresh = (
        jnp.einsum("sqhd,skd->sqhk", paired, fresh_keys, preferred_element_type=jnp.float32)
        * SCORE_SCALE
    )
    causal = jnp.arange(2)[:, None] >= jnp.arange(2)[None, :]
    fresh = jnp.where(causal[None, :, None, :], fresh, MASKED)
    top = jnp.maximum(jnp.max(scores, axis=3), jnp.max(fresh, axis=3))[..., None]
    weights = jnp.exp(scores - top)
    fresh_weights = jnp.exp(fresh - top)
    total = jnp.sum(weights, axis=3) + jnp.sum(fresh_weights, axis=3)
    summed = jnp.einsum(
        "sqhp,spd->sqhd",
        weights.astype(jnp.bfloat16),
        latent_cache[:, :, :LAT],
        preferred_element_type=jnp.float32,
    )
    summed = summed + jnp.einsum(
        "sqhk,skd->sqhd",
        fresh_weights.astype(jnp.bfloat16),
        fresh_keys[:, :, :LAT],
        preferred_element_type=jnp.float32,
    )
    attended = (
        (summed / total[..., None]).astype(jnp.bfloat16).reshape(seq_count * 2, local_heads, LAT)
    )
    by_head = lax.all_to_all(attended, "tensor", split_axis=1, concat_axis=0, tiled=True)
    head_values = jnp.einsum(
        "thl,hlv->thv", by_head, value_proj, preferred_element_type=jnp.float32
    ).astype(jnp.bfloat16)
    head_values = head_values.reshape(
        head_values.shape[0], head_values.shape[1] * head_values.shape[2]
    )
    all_values = lax.all_gather(head_values, "dp", axis=0, tiled=True)
    owners = down_pack[:, hidden_slice, :capacity].astype(jnp.int32).reshape(n_slices * capacity)
    down_pack = down_pack[:, :hidden_slice].reshape(n_slices * hidden_slice, pack_width)
    down_w = down_pack[:, :col_width]
    left_w = down_pack[:, col_width:].reshape(n_slices * hidden_slice, tenants, rank)
    down_w, left_w, owners, all_values = lax.optimization_barrier(
        (down_w, left_w, owners, all_values)
    )
    partial = jnp.dot(all_values, out_proj, preferred_element_type=jnp.float32)
    half = partial.shape[0] // 2
    role_idx = lax.axis_index("role")
    keep = lax.dynamic_slice_in_dim(partial, role_idx * half, half, 0)
    give = lax.dynamic_slice_in_dim(partial, (1 - role_idx) * half, half, 0)
    partial = keep + lax.ppermute(give.astype(jnp.bfloat16), "role", [(0, 1), (1, 0)]).astype(
        jnp.float32
    )
    n_tensor = lax.axis_size("tensor")
    partial = partial.reshape(n_tensor, partial.shape[0] // n_tensor, partial.shape[1])
    partial = lax.all_to_all(
        partial.astype(jnp.bfloat16), "tensor", split_axis=0, concat_axis=0, tiled=True
    )
    attention = jnp.sum(partial.astype(jnp.float32), axis=0)
    mixed_in = lax.optimization_barrier(
        (residual.astype(jnp.float32) + attention).astype(jnp.bfloat16)
    )
    n_dp = lax.axis_size("dp")
    spread = jnp.broadcast_to(mixed_in[None], (n_dp,) + mixed_in.shape)
    full_rows = lax.all_to_all(spread, "dp", split_axis=0, concat_axis=0, tiled=True)
    full_rows = full_rows.reshape(-1, group_rows, mixed_in.shape[1])
    full_rows = jnp.transpose(full_rows, (1, 0, 2)).reshape(group_rows, model_width)
    normed = rms_rows(full_rows, norm_gain)
    picked = jnp.dot(mine.astype(jnp.bfloat16), normed, preferred_element_type=jnp.float32).astype(
        jnp.bfloat16
    )
    collected_rows = lax.all_gather(picked, RT, axis=0, tiled=True)
    gate_scores = jnp.dot(collected_rows, expert_gate_weight[0], preferred_element_type=jnp.float32)
    upper_bound = jnp.dot(collected_rows, expert_up_weight[0], preferred_element_type=jnp.float32)
    hidden = (jax.nn.silu(gate_scores) * upper_bound).astype(jnp.bfloat16)
    gathered = lax.all_gather(hidden, RT, axis=0, tiled=False)
    down_w = down_w.reshape(n_slices, hidden_slice, col_width)
    left_w = left_w.reshape(n_slices, hidden_slice, tenants, rank)
    base_output = jnp.einsum("jsh,jhc->sc", gathered, down_w, preferred_element_type=jnp.float32)
    owner_mask = (owners[:, None] == jnp.arange(TEN, dtype=jnp.int32)[None, :]).astype(jnp.float32)
    mixing = (
        jnp.einsum("jsf,jftr->str", gathered, left_w, preferred_element_type=jnp.float32)
        * owner_mask[:, :, None]
    )
    delta = jnp.einsum(
        "str,trd->sd", mixing, right_w.astype(jnp.float32), precision=lax.Precision.HIGHEST
    )
    expert_out = (base_output - delta).astype(jnp.bfloat16)
    expert_out = expert_out.reshape(n_slices, capacity, col_width)
    by_group = lax.all_to_all(expert_out, RT, split_axis=0, concat_axis=0, tiled=True)
    by_expert = lax.all_to_all(by_group, "dp", split_axis=0, concat_axis=0, tiled=True)
    chosen = (routes[:, :, None] == labels[None, None, :]).astype(jnp.float32)
    gate_of = jnp.sum(gate_values[:, :, None] * chosen, axis=1)
    weighting = table.astype(jnp.float32) * gate_of.T[:, None, :]
    expert_part = jnp.einsum(
        "ecg,ecd->gd", weighting, by_expert.astype(jnp.float32), precision=lax.Precision.HIGHEST
    )
    return (mixed_in.astype(jnp.float32) + expert_part).astype(jnp.bfloat16)


def solution(mesh):
    placed = (
        P(("dp", "tensor"), "role", None),
        P(("dp", "tensor"), None, None),
        P(("dp", "tensor"), None),
        P(("dp", "tensor")),
        P(("role", "tensor"), None, None),
        P(("role", "tensor"), "dp"),
        P(("role", "tensor"), "dp"),
        P(),
        P(("role", "tensor"), None),
        P(("role", "tensor"), None),
        P(("role", "tensor")),
        P("dp", None, ("role", "tensor")),
        P("dp", None, ("role", "tensor")),
        P("dp", ("role", "tensor"), None),
        P(None, "dp", ("role", "tensor"), None),
        P(None, "dp", None, None),
    )
    return jax.shard_map(
        local, mesh=mesh, in_specs=placed, out_specs=P(("role", "tensor"), "dp"), check_vma=False
    )
```

profile of v0, /device:TPU:32, one launch (start us, length us, event | category | flops | bytes accessed | tf_op | source)
XLA Modules:
  0.0 349.5 jit_solution(5170644350469607524)
XLA Ops:
  8.2 3.9 %fusion.8 = (f32[4,2,64]{2,1,0:T(2,128)S(1)}, f32[4,2,64,1024]{3,2,1,0:T(8,128)S(1)}) fusion(pred[4,1024]{1,0:T(4,128)(4,1)S(1)} %iota_compare_fusion.3, bf16[4,2,64,576]{3,2,1,0:T(8,128)(2,1)} %bitcast.125, bf16[4,1024,576]{1,2,0:T(8,128)(2,1)} %param.19), kind=kOutput, calls=%fused_computation.14 | convolution fusion | flops 605552128 | bytes 7411712 | tf_op jit(solution)/shard_map/sqhd,spd->sqhp/dot_general | solution.py:76
  13.2 2.5 fusion.2
  15.8 1.6 fusion.18
  18.5 8.6 %all-to-all-start.1 = ((bf16[8,64,512]{2,0,1:T(8,128)(2,1)}), bf16[8,64,512]{2,0,1:T(8,128)(2,1)S(1)}, u32[]{:S(2)}, u32[]{:S(2)}) async-start(bf16[8,64,512]{2,0,1:T(8,128)(2,1)} %copy.75), calls=%async_computation.1 | async-start | bytes 1048576 | tf_op jit(solution)/shard_map/all_to_all | solution.py:107
  27.7 3.9 %copy.70 = bf16[1,128,7168]{1,2,0:T(8,128)(2,1)} copy(bf16[1,128,7168]{2,1,0:T(8,128)(2,1)} %param.31) | data formatting | bytes 3670016 | tf_op args[13]
  33.1 3.5 pad_maximum_fusion
  36.6 6.3 %copy.72 = bf16[16,136,640]{2,1,0:T(8,128)(2,1)} copy(bf16[16,136,640]{1,2,0:T(8,128)(2,1)} %pad_maximum_fusion) | data formatting | bytes 5570560 | tf_op jit(solution)/shard_map/concatenate | solution.py:69
  43.1 6.9 %all-to-all-start = ((bf16[16,136,640]{2,1,0:T(8,128)(2,1)}), bf16[16,136,640]{2,1,0:T(8,128)(2,1)}, u32[]{:S(2)}, u32[]{:S(2)}) async-start(bf16[16,136,640]{2,1,0:T(8,128)(2,1)} %copy.72), calls=%async_computation | async-start | bytes 5570560 | tf_op jit(solution)/shard_map/all_to_all | solution.py:70
  50.1 1.5 fusion.27
  52.4 60.9 %all-to-all-done = bf16[16,136,640]{2,1,0:T(8,128)(2,1)} async-done(((bf16[16,136,640]{2,1,0:T(8,128)(2,1)}), bf16[16,136,640]{2,1,0:T(8,128)(2,1)}, u32[]{:S(2)}, u32[]{:S(2)}) %all-to-all-start) | async-done | bytes 2785312 | tf_op jit(solution)/shard_map/all_to_all | solution.py:70
  113.2 2.0 slice.40
  118.1 2.2 copy.73
  121.2 3.0 fusion.63
  126.0 1.6 collective-permute-done
  127.6 2.2 add_convert_fusion
  131.0 21.8 %all_to_all.43 = bf16[8,64,448]{2,1,0:T(8,128)(2,1)S(1)} all-to-all(bf16[8,64,448]{2,1,0:T(8,128)(2,1)S(1)} %bitcast.123), channel_id=1, replica_groups=mesh['role'=2,'dp'=16,'tensor'=8] {'tensor'}, dimensions={0} | all-to-all | bytes 917504 | tf_op jit(solution)/shard_map/all_to_all | solution.py:132
  154.6 7.1 %all-to-all-start.3 = ((bf16[16,64,448]{2,1,0:T(8,128)(2,1)}), bf16[16,64,448]{2,1,0:T(8,128)(2,1)}, u32[]{:S(2)}, u32[]{:S(2)}) async-start(bf16[16,64,448]{2,1,0:T(8,128)(2,1)} %broadcast_in_dim.39), calls=%async_computation.3 | async-start | bytes 2097152 | tf_op jit(solution)/shard_map/all_to_all | solution.py:141
  162.0 14.8 %all-to-all-done.3 = bf16[16,64,448]{2,1,0:T(8,128)(2,1)} async-done(((bf16[16,64,448]{2,1,0:T(8,128)(2,1)}), bf16[16,64,448]{2,1,0:T(8,128)(2,1)}, u32[]{:S(2)}, u32[]{:S(2)}) %all-to-all-start.3) | async-done | bytes 917536 | tf_op jit(solution)/shard_map/all_to_all | solution.py:141
  176.8 1.6 fusion.5
  178.4 1.6 fusion.31
  179.9 1.5 copy.79
  181.5 2.9 convert_element_type.133
  184.4 2.3 convolution_convert_fusion
  186.8 53.2 %all-gather.7.cloned.1.call-done = bf16[640,7168]{1,0:T(8,128)(2,1)} async-done(((bf16[40,7168]{1,0:T(8,128)(2,1)}), bf16[640,7168]{1,0:T(8,128)(2,1)}) %all-gather.7.cloned.1.call-update) | async-done | bytes 9175056 | tf_op jit(solution)/shard_map/all_gather | solution.py:148
  239.9 6.8 %fusion.11 = f32[640,128]{1,0:T(8,128)S(1)} fusion(bf16[640,7168]{1,0:T(8,128)(2,1)} %all-gather.7.cloned.1.call-done, bf16[1,7168,128]{2,1,0:T(8,128)(2,1)} %param.29), kind=kOutput, calls=%fused_computation.17 | convolution fusion | flops 1174405120 | bytes 11337728 | tf_op jit(solution)/shard_map/dot_general | solution.py:149
  247.2 3.2 fusion.23
  251.0 39.7 %all-gather.9.cloned.1.call-done = bf16[10240,128]{1,0:T(8,128)(2,1)} async-done(((bf16[640,128]{1,0:T(8,128)(2,1)}), bf16[10240,128]{1,0:T(8,128)(2,1)}) %all-gather.9.cloned.1.call-update) | async-done | bytes 2621456 | tf_op jit(solution)/shard_map/all_gather | solution.py:152
  290.8 2.9 fusion.19
  294.5 2.4 fusion.17
  298.3 24.5 %all_to_all.44 = bf16[16,40,448]{2,1,0:T(8,128)(2,1)} all-to-all(bf16[16,40,448]{2,1,0:T(8,128)(2,1)S(1)} %bitcast.120), channel_id=1, replica_groups=mesh['role'=2,'dp'=16,'tensor'=8] {'role','tensor'}, dimensions={0} | all-to-all | bytes 1146880 | tf_op jit(solution)/shard_map/all_to_all | solution.py:166
  322.9 6.8 %all-to-all-start.5 = ((bf16[16,40,448]{2,1,0:T(8,128)(2,1)}), bf16[16,40,448]{2,1,0:T(8,128)(2,1)S(1)}, u32[]{:S(2)}, u32[]{:S(2)}) async-start(bf16[16,40,448]{2,1,0:T(8,128)(2,1)} %all_to_all.44), calls=%async_computation.5 | async-start | bytes 1310720 | tf_op jit(solution)/shard_map/all_to_all | solution.py:167
  329.7 12.1 %all-to-all-done.5 = bf16[16,40,448]{2,1,0:T(8,128)(2,1)S(1)} async-done(((bf16[16,40,448]{2,1,0:T(8,128)(2,1)}), bf16[16,40,448]{2,1,0:T(8,128)(2,1)S(1)}, u32[]{:S(2)}, u32[]{:S(2)}) %all-to-all-start.5) | async-done | bytes 573472 | tf_op jit(solution)/shard_map/all_to_all | solution.py:167
  (90 shorter events, 20.3 us)
Async XLA Ops:
  6.5 287.1 %copy-start = (bf16[3,1,64,7168]{3,2,1,0:T(8,128)(2,1)S(1)}, bf16[3,1,64,7168]{3,2,1,0:T(8,128)(2,1)}, u32[]{:S(2)}) copy-start(bf16[3,1,64,7168]{3,2,1,0:T(8,128)(2,1)} %param.33) | copy-start | bytes 8257540
  8.1 5.0 %slice-start = ((s8[4718592]{0:T(1024)(128)(4,1)}), s8[4194304]{0:T(1024)(128)(4,1)S(1)}, s32[]{:S(2)}) async-start(s8[4718592]{0:T(1024)(128)(4,1)} %bitcast.118), calls=%async_computation.9 | async-start | bytes 8388608
  8.1 4.0 %copy-start.5 = (bf16[8,64,576]{2,1,0:T(8,128)(2,1)S(1)}, bf16[8,64,576]{2,1,0:T(8,128)(2,1)}, u32[]{:S(2)}) copy-start(bf16[8,64,576]{2,1,0:T(8,128)(2,1)} %param.18) | copy-start | bytes 1769476
  8.2 5.0 %slice-start.1 = ((s8[4718592]{0:T(1024)(128)(4,1)}), s8[524288]{0:T(1024)(128)(4,1)S(1)}, s32[]{:S(2)}) async-start(s8[4718592]{0:T(1024)(128)(4,1)} %bitcast.118), calls=%async_computation.10 | async-start | bytes 1048576
  13.2 2.5 copy-start.10
  15.8 11.3 %copy-start.11 = (s32[64,8]{0,1:T(8,128)S(1)}, s32[64,8]{0,1:T(8,128)}, u32[]{:S(2)}) copy-start(s32[64,8]{0,1:T(8,128)} %param.26) | copy-start | bytes 6148
  17.4 10.1 %copy-start.15 = (s32[64]{0:T(128)S(1)}, s32[64]{0:T(128)}, u32[]{:S(2)}) copy-start(s32[64]{0:T(128)} %param.28) | copy-start | bytes 772
  18.5 24.6 %all-to-all-start.1 = ((bf16[8,64,512]{2,0,1:T(8,128)(2,1)}), bf16[8,64,512]{2,0,1:T(8,128)(2,1)S(1)}, u32[]{:S(2)}, u32[]{:S(2)}) async-start(bf16[8,64,512]{2,0,1:T(8,128)(2,1)} %copy.75), calls=%async_computation.1 | async-start | bytes 1048576 | tf_op jit(solution)/shard_map/all_to_all | solution.py:107
  27.1 4.5 %copy-start.9 = (bf16[3,1,128,64]{2,3,1,0:T(8,128)(2,1)S(1)}, bf16[3,1,128,64]{2,3,1,0:T(8,128)(2,1)}, u32[]{:S(2)}) copy-start(bf16[3,1,128,64]{2,3,1,0:T(8,128)(2,1)} %param.32) | copy-start | bytes 147460
  31.6 1.5 copy-start.1
  43.1 70.1 %all-to-all-start = ((bf16[16,136,640]{2,1,0:T(8,128)(2,1)}), bf16[16,136,640]{2,1,0:T(8,128)(2,1)}, u32[]{:S(2)}, u32[]{:S(2)}) async-start(bf16[16,136,640]{2,1,0:T(8,128)(2,1)} %copy.72), calls=%async_computation | async-start | bytes 5570560 | tf_op jit(solution)/shard_map/all_to_all | solution.py:70
  50.1 71.1 %all-gather.5.cloned.1.call-start = ((), (), s32[]{:S(2)}) async-start(), calls=%async_computation.6 | async-start | bytes 2228224 | tf_op jit(solution)/shard_map/all_gather | solution.py:114
  124.2 1.3 copy-start.3
  125.5 2.1 collective-permute-start
  126.0 26.9 %copy-start.8 = (bf16[64,448]{1,0:T(8,128)(2,1)S(1)}, bf16[64,448]{1,0:T(8,128)(2,1)}, u32[]{:S(2)}) copy-start(bf16[64,448]{1,0:T(8,128)(2,1)} %param.24) | copy-start | bytes 172036
  152.8 9.2 %copy-start.13 = (bf16[7168]{0:T(1024)(128)(2,1)S(1)}, bf16[7168]{0:T(1024)(128)(2,1)}, u32[]{:S(2)}) copy-start(bf16[7168]{0:T(1024)(128)(2,1)} %param.25) | copy-start | bytes 43012
  152.9 0.6 copy-start.6
  154.6 22.2 %all-to-all-start.3 = ((bf16[16,64,448]{2,1,0:T(8,128)(2,1)}), bf16[16,64,448]{2,1,0:T(8,128)(2,1)}, u32[]{:S(2)}, u32[]{:S(2)}) async-start(bf16[16,64,448]{2,1,0:T(8,128)(2,1)} %broadcast_in_dim.39), calls=%async_computation.3 | async-start | bytes 2097152 | tf_op jit(solution)/shard_map/all_to_all | solution.py:141
  161.7 78.2 %all-gather.7.cloned.1.call-start = ((), (), s32[]{:S(2)}) async-start(), calls=%async_computation.7 | async-start | bytes 9748480 | tf_op jit(solution)/shard_map/all_gather | solution.py:148
  186.7 104.0 %all-gather.9.cloned.1.call-start = ((), (), s32[]{:S(2)}) async-start(), calls=%async_computation.8 | async-start | bytes 2785280 | tf_op jit(solution)/shard_map/all_gather | solution.py:152
  239.9 6.8 %copy-start.16 = (bf16[640,7168]{1,0:T(8,128)(2,1)S(1)}, bf16[640,7168]{1,0:T(8,128)(2,1)}, u32[]{:S(2)}) copy-start(bf16[640,7168]{1,0:T(8,128)(2,1)} %all-gather.7.cloned.1.call-done) | copy-start | bytes 27525124
  239.9 7.2 %copy-start.18 = (bf16[1,7168,128]{2,1,0:T(8,128)(2,1)S(1)}, bf16[1,7168,128]{2,1,0:T(8,128)(2,1)}, u32[]{:S(2)}) copy-start(bf16[1,7168,128]{2,1,0:T(8,128)(2,1)} %param.30) | copy-start | bytes 5505028
  247.2 43.6 %copy-start.4 = (bf16[2048,192]{0,1:T(8,128)(2,1)S(1)}, bf16[2048,192]{0,1:T(8,128)(2,1)}, u32[]{:S(2)}) copy-start(bf16[2048,192]{0,1:T(8,128)(2,1)} %copy.73) | copy-start | bytes 2359300
  290.8 3.8 %copy-start.2 = (bf16[2048,448]{1,0:T(8,128)(2,1)S(1)}, bf16[2048,448]{1,0:T(8,128)(2,1)}, u32[]{:S(2)}) copy-start(bf16[2048,448]{1,0:T(8,128)(2,1)} %slice.41) | copy-start | bytes 5505028
  290.8 3.8 %copy-start.17 = (bf16[10240,128]{1,0:T(8,128)(2,1)S(1)}, bf16[10240,128]{1,0:T(8,128)(2,1)}, u32[]{:S(2)}) copy-start(bf16[10240,128]{1,0:T(8,128)(2,1)} %all-gather.9.cloned.1.call-done) | copy-start | bytes 7864324
  297.0 32.7 %copy-start.12 = (s32[64,8]{0,1:T(8,128)S(1)}, s32[64,8]{0,1:T(8,128)}, u32[]{:S(2)}) copy-start(s32[64,8]{0,1:T(8,128)} %param.26) | copy-start | bytes 6148
  297.0 32.7 %copy-start.14 = (f32[64,8]{0,1:T(8,128)S(1)}, f32[64,8]{0,1:T(8,128)}, u32[]{:S(2)}) copy-start(f32[64,8]{0,1:T(8,128)} %param.27) | copy-start | bytes 6148
  297.0 44.9 %copy-start.7 = (bf16[64,448]{1,0:T(8,128)(2,1)S(1)}, bf16[64,448]{1,0:T(8,128)(2,1)}, u32[]{:S(2)}) copy-start(bf16[64,448]{1,0:T(8,128)(2,1)} %copy-done.6) | copy-start | bytes 172036
  322.9 19.0 %all-to-all-start.5 = ((bf16[16,40,448]{2,1,0:T(8,128)(2,1)}), bf16[16,40,448]{2,1,0:T(8,128)(2,1)S(1)}, u32[]{:S(2)}, u32[]{:S(2)}) async-start(bf16[16,40,448]{2,1,0:T(8,128)(2,1)} %all_to_all.44), calls=%async_computation.5 | async-start | bytes 1310720 | tf_op jit(solution)/shard_map/all_to_all | solution.py:167
Sparse Core Ops, SparseCore 0:
  53.3 51.1 all-gather.4
  186.8 53.0 all-gather.6
  250.5 40.1 all-gather.8
where the time goes:
time: 351 us; the launch traced here: 350 us
  waiting for transfers between devices  183 us (52%)
  blocking collectives  46.3 us (13%)
  matrix products  32.5 us (9%)
  local copies, waits for them, and re-layouts  32.1 us (9%)
  starting transfers between devices  30.2 us (9%)
  between operations  13.5 us (4%)
  other arithmetic  12.3 us (4%)
    all_to_all x1, waiting for transfers between devices, local(): lax.all_to_all(down_pack, RT, split_axis=0, concat_axis=0, tiled=True)  60.9 us
    all_gather x1, waiting for transfers between devices, local(): collected_rows = lax.all_gather(picked, RT, axis=0, tiled=True)  53.2 us
    all_gather x1, waiting for transfers between devices, local(): gathered = lax.all_gather(hidden, RT, axis=0, tiled=False)  39.7 us
    all_to_all x1, blocking collectives, local(): lax.all_to_all(expert_out, RT, split_axis=0, concat_axis=0, tiled=True)  24.5 us
    all_to_all x1, blocking collectives, local(): lax.all_to_all(partial.astype(jnp.bfloat16), 'tensor', split_axis=0, conc...  21.8 us
    all_to_all x1, waiting for transfers between devices, local(): lax.all_to_all(spread, 'dp', split_axis=0, concat_axis=0, tiled=True)  14.8 us
    all_to_all x1, waiting for transfers between devices, local(): lax.all_to_all(by_group, 'dp', split_axis=0, concat_axis=0, tiled=True)  12.1 us
    all_to_all x1, starting transfers between devices, local(): lax.all_to_all(attended, 'tensor', split_axis=1, concat_axis=0, tiled=True)  8.57 us
  transfers between devices with their start and end apart: 8, of which 7 were waited for; matrix products, arithmetic and copies ran while one was open for 7% of the time, Pallas kernels for 0%

commit v1 on v0

--- a/solution.py
+++ b/solution.py
@@ -145,7 +145,9 @@
     picked = jnp.dot(mine.astype(jnp.bfloat16), normed, preferred_element_type=jnp.float32).astype(
         jnp.bfloat16
     )
-    collected_rows = lax.all_gather(picked, RT, axis=0, tiled=True)
+    collected_rows = jnp.concatenate(
+        lax.all_to_all(jnp.stack([picked] * lax.axis_size(RT)), RT, 0, 0), axis=0
+    )
     gate_scores = jnp.dot(collected_rows, expert_gate_weight[0], preferred_element_type=jnp.float32)
     upper_bound = jnp.dot(collected_rows, expert_up_weight[0], preferred_element_type=jnp.float32)
     hidden = (jax.nn.silu(gate_scores) * upper_bound).astype(jnp.bfloat16)

time: 351 us -> 494 us (1.41)
  blocking collectives: 46.3 us -> 253 us
  waiting for transfers between devices: 183 us -> 123 us
  matrix products: 32.5 us -> 27.4 us
    all_to_all x0 -> x1, blocking collectives: none -> 207 us  [local(): lax.all_to_all(jnp.stack([picked] * lax.axis_size(RT)), RT, 0, 0)]
    all_gather x1 -> x0, waiting for transfers between devices: 53.2 us -> none  [local(): collected_rows = lax.all_gather(picked, RT, axis=0, tiled=True)]
    all_gather x1, waiting for transfers between devices: 39.7 us -> 33.6 us  [local(): gathered = lax.all_gather(hidden, RT, axis=0, tiled=False)]
  transfers between devices with their start and end apart: 8 -> 7, of which waited for: 7 -> 6; matrix products, arithmetic and copies ran while one was open for 7% -> 5% of each run, Pallas kernels for 0% -> 0%
where the time goes in v1:
time: 494 us; the launch traced here: 493 us
  blocking collectives  253 us (51%)
  waiting for transfers between devices  123 us (25%)
  local copies, waits for them, and re-layouts  32.9 us (7%)
  starting transfers between devices  30.1 us (6%)
  matrix products  27.4 us (6%)
  between operations  13.8 us (3%)
  other arithmetic  12.3 us (2%)
    all_to_all x1, blocking collectives, local(): lax.all_to_all(jnp.stack([picked] * lax.axis_size(RT)), RT, 0, 0)  207 us
    all_to_all x1, waiting for transfers between devices, local(): lax.all_to_all(down_pack, RT, split_axis=0, concat_axis=0, tiled=True)  60.9 us
    all_gather x1, waiting for transfers between devices, local(): gathered = lax.all_gather(hidden, RT, axis=0, tiled=False)  33.6 us
    all_to_all x1, blocking collectives, local(): lax.all_to_all(expert_out, RT, split_axis=0, concat_axis=0, tiled=True)  24.5 us
    all_to_all x1, blocking collectives, local(): lax.all_to_all(partial.astype(jnp.bfloat16), 'tensor', split_axis=0, conc...  21.8 us
    all_to_all x1, waiting for transfers between devices, local(): lax.all_to_all(spread, 'dp', split_axis=0, concat_axis=0, tiled=True)  14.8 us
    all_to_all x1, waiting for transfers between devices, local(): lax.all_to_all(by_group, 'dp', split_axis=0, concat_axis=0, tiled=True)  12.1 us
  transfers between devices with their start and end apart: 7, of which 6 were waited for; matrix products, arithmetic and copies ran while one was open for 5% of the time, Pallas kernels for 0%

profile of v1, /device:TPU:32, one launch (start us, length us, event | category | flops | bytes accessed | tf_op | source)
XLA Modules:
  0.0 493.3 jit_solution(2510581231008487154)
XLA Ops:
  8.2 3.9 fusion.8
  13.2 2.5 fusion.2
  15.8 1.6 fusion.18
  18.5 8.6 %all-to-all-start.1 = ((bf16[8,64,512]{2,0,1:T(8,128)(2,1)}), bf16[8,64,512]{2,0,1:T(8,128)(2,1)S(1)}, u32[]{:S(2)}, u32[]{:S(2)}) async-start(bf16[8,64,512]{2,0,1:T(8,128)(2,1)} %copy.75), calls=%async_computation.1 | async-start | bytes 1048576 | tf_op jit(solution)/shard_map/all_to_all | solution.py:107
  27.6 3.9 copy.70
  33.0 3.5 pad_maximum_fusion
  36.5 6.2 %copy.72 = bf16[16,136,640]{2,1,0:T(8,128)(2,1)} copy(bf16[16,136,640]{1,2,0:T(8,128)(2,1)} %pad_maximum_fusion) | data formatting | bytes 5570560 | tf_op jit(solution)/shard_map/concatenate | solution.py:69
  43.1 6.9 %all-to-all-start = ((bf16[16,136,640]{2,1,0:T(8,128)(2,1)}), bf16[16,136,640]{2,1,0:T(8,128)(2,1)}, u32[]{:S(2)}, u32[]{:S(2)}) async-start(bf16[16,136,640]{2,1,0:T(8,128)(2,1)} %copy.72), calls=%async_computation | async-start | bytes 5570560 | tf_op jit(solution)/shard_map/all_to_all | solution.py:70
  50.0 1.5 fusion.27
  52.3 60.9 %all-to-all-done = bf16[16,136,640]{2,1,0:T(8,128)(2,1)} async-done(((bf16[16,136,640]{2,1,0:T(8,128)(2,1)}), bf16[16,136,640]{2,1,0:T(8,128)(2,1)}, u32[]{:S(2)}, u32[]{:S(2)}) %all-to-all-start) | async-done | bytes 2785312 | tf_op jit(solution)/shard_map/all_to_all | solution.py:70
  113.2 2.0 slice.40
  116.6 1.5 slice.42
  118.2 2.2 copy.73
  121.3 3.0 fusion.63
  126.1 1.6 collective-permute-done
  127.6 2.2 add_convert_fusion
  131.1 21.8 %all_to_all.48 = bf16[8,64,448]{2,1,0:T(8,128)(2,1)S(1)} all-to-all(bf16[8,64,448]{2,1,0:T(8,128)(2,1)S(1)} %bitcast.126), channel_id=1, replica_groups=mesh['role'=2,'dp'=16,'tensor'=8] {'tensor'}, dimensions={0} | all-to-all | bytes 917504 | tf_op jit(solution)/shard_map/all_to_all | solution.py:132
  154.7 7.1 %all-to-all-start.3 = ((bf16[16,64,448]{2,1,0:T(8,128)(2,1)}), bf16[16,64,448]{2,1,0:T(8,128)(2,1)}, u32[]{:S(2)}, u32[]{:S(2)}) async-start(bf16[16,64,448]{2,1,0:T(8,128)(2,1)} %broadcast_in_dim.39), calls=%async_computation.3 | async-start | bytes 2097152 | tf_op jit(solution)/shard_map/all_to_all | solution.py:141
  162.1 14.8 %all-to-all-done.3 = bf16[16,64,448]{2,1,0:T(8,128)(2,1)} async-done(((bf16[16,64,448]{2,1,0:T(8,128)(2,1)}), bf16[16,64,448]{2,1,0:T(8,128)(2,1)}, u32[]{:S(2)}, u32[]{:S(2)}) %all-to-all-start.3) | async-done | bytes 917536 | tf_op jit(solution)/shard_map/all_to_all | solution.py:141
  176.9 1.6 fusion.5
  178.5 1.6 fusion.31
  180.0 1.6 copy.79
  181.6 2.9 convert_element_type.133
  187.1 207.1 %all_to_all.49 = bf16[16,40,7168]{2,1,0:T(8,128)(2,1)S(1)} all-to-all(bf16[16,40,7168]{2,1,0:T(8,128)(2,1)S(1)} %stack.2), channel_id=1, replica_groups=mesh['role'=2,'dp'=16,'tensor'=8] {'role','tensor'}, dimensions={0} | all-to-all | bytes 18350080 | tf_op jit(solution)/shard_map/all_to_all | solution.py:149
  394.2 2.5 fusion.11
  396.8 3.2 fusion.23
  400.6 33.6 %all-gather.6.cloned.1.call-done = bf16[10240,128]{1,0:T(8,128)(2,1)} async-done(((bf16[640,128]{1,0:T(8,128)(2,1)}), bf16[10240,128]{1,0:T(8,128)(2,1)}) %all-gather.6.cloned.1.call-update) | async-done | bytes 2621456 | tf_op jit(solution)/shard_map/all_gather | solution.py:154
  434.2 2.9 fusion.19
  438.0 2.4 fusion.17
  441.8 24.5 %all_to_all.50 = bf16[16,40,448]{2,1,0:T(8,128)(2,1)} all-to-all(bf16[16,40,448]{2,1,0:T(8,128)(2,1)S(1)} %bitcast.123), channel_id=1, replica_groups=mesh['role'=2,'dp'=16,'tensor'=8] {'role','tensor'}, dimensions={0} | all-to-all | bytes 1146880 | tf_op jit(solution)/shard_map/all_to_all | solution.py:168
  466.3 6.8 %all-to-all-start.6 = ((bf16[16,40,448]{2,1,0:T(8,128)(2,1)}), bf16[16,40,448]{2,1,0:T(8,128)(2,1)S(1)}, u32[]{:S(2)}, u32[]{:S(2)}) async-start(bf16[16,40,448]{2,1,0:T(8,128)(2,1)} %all_to_all.50), calls=%async_computation.6 | async-start | bytes 1310720 | tf_op jit(solution)/shard_map/all_to_all | solution.py:169
  473.2 12.1 %all-to-all-done.6 = bf16[16,40,448]{2,1,0:T(8,128)(2,1)S(1)} async-done(((bf16[16,40,448]{2,1,0:T(8,128)(2,1)}), bf16[16,40,448]{2,1,0:T(8,128)(2,1)S(1)}, u32[]{:S(2)}, u32[]{:S(2)}) %all-to-all-start.6) | async-done | bytes 573472 | tf_op jit(solution)/shard_map/all_to_all | solution.py:169
  (89 shorter events, 21.0 us)
Async XLA Ops:
  6.5 430.6 %copy-start = (bf16[3,1,64,7168]{3,2,1,0:T(8,128)(2,1)S(1)}, bf16[3,1,64,7168]{3,2,1,0:T(8,128)(2,1)}, u32[]{:S(2)}) copy-start(bf16[3,1,64,7168]{3,2,1,0:T(8,128)(2,1)} %param.33) | copy-start | bytes 8257540
  8.1 5.0 %slice-start = ((s8[4718592]{0:T(1024)(128)(4,1)}), s8[4194304]{0:T(1024)(128)(4,1)S(1)}, s32[]{:S(2)}) async-start(s8[4718592]{0:T(1024)(128)(4,1)} %bitcast.121), calls=%async_computation.9 | async-start | bytes 8388608
  8.1 4.0 copy-start.5
  8.2 5.0 %slice-start.1 = ((s8[4718592]{0:T(1024)(128)(4,1)}), s8[524288]{0:T(1024)(128)(4,1)S(1)}, s32[]{:S(2)}) async-start(s8[4718592]{0:T(1024)(128)(4,1)} %bitcast.121), calls=%async_computation.10 | async-start | bytes 1048576
  13.2 2.5 copy-start.10
  15.8 11.3 %copy-start.11 = (s32[64,8]{0,1:T(8,128)S(1)}, s32[64,8]{0,1:T(8,128)}, u32[]{:S(2)}) copy-start(s32[64,8]{0,1:T(8,128)} %param.26) | copy-start | bytes 6148
  17.4 10.0 %copy-start.15 = (s32[64]{0:T(128)S(1)}, s32[64]{0:T(128)}, u32[]{:S(2)}) copy-start(s32[64]{0:T(128)} %param.28) | copy-start | bytes 772
  18.5 24.6 %all-to-all-start.1 = ((bf16[8,64,512]{2,0,1:T(8,128)(2,1)}), bf16[8,64,512]{2,0,1:T(8,128)(2,1)S(1)}, u32[]{:S(2)}, u32[]{:S(2)}) async-start(bf16[8,64,512]{2,0,1:T(8,128)(2,1)} %copy.75), calls=%async_computation.1 | async-start | bytes 1048576 | tf_op jit(solution)/shard_map/all_to_all | solution.py:107
  27.1 4.5 copy-start.9
  31.5 1.5 copy-start.1
  43.1 70.1 %all-to-all-start = ((bf16[16,136,640]{2,1,0:T(8,128)(2,1)}), bf16[16,136,640]{2,1,0:T(8,128)(2,1)}, u32[]{:S(2)}, u32[]{:S(2)}) async-start(bf16[16,136,640]{2,1,0:T(8,128)(2,1)} %copy.72), calls=%async_computation | async-start | bytes 5570560 | tf_op jit(solution)/shard_map/all_to_all | solution.py:70
  50.0 71.3 %all-gather.4.cloned.1.call-start = ((), (), s32[]{:S(2)}) async-start(), calls=%async_computation.7 | async-start | bytes 2228224 | tf_op jit(solution)/shard_map/all_gather | solution.py:114
  124.3 1.3 copy-start.3
  125.6 2.1 collective-permute-start
  126.1 26.9 %copy-start.8 = (bf16[64,448]{1,0:T(8,128)(2,1)S(1)}, bf16[64,448]{1,0:T(8,128)(2,1)}, u32[]{:S(2)}) copy-start(bf16[64,448]{1,0:T(8,128)(2,1)} %param.24) | copy-start | bytes 172036
  152.9 9.1 %copy-start.13 = (bf16[7168]{0:T(1024)(128)(2,1)S(1)}, bf16[7168]{0:T(1024)(128)(2,1)}, u32[]{:S(2)}) copy-start(bf16[7168]{0:T(1024)(128)(2,1)} %param.25) | copy-start | bytes 43012
  153.0 0.6 copy-start.6
  154.7 22.2 %all-to-all-start.3 = ((bf16[16,64,448]{2,1,0:T(8,128)(2,1)}), bf16[16,64,448]{2,1,0:T(8,128)(2,1)}, u32[]{:S(2)}, u32[]{:S(2)}) async-start(bf16[16,64,448]{2,1,0:T(8,128)(2,1)} %broadcast_in_dim.39), calls=%async_computation.3 | async-start | bytes 2097152 | tf_op jit(solution)/shard_map/all_to_all | solution.py:141
  161.8 272.4 %all-gather.6.cloned.1.call-start = ((), (), s32[]{:S(2)}) async-start(), calls=%async_computation.8 | async-start | bytes 2785280 | tf_op jit(solution)/shard_map/all_gather | solution.py:154
  187.1 207.1 %copy-start.17 = (bf16[1,7168,128]{2,1,0:T(8,128)(2,1)S(1)}, bf16[1,7168,128]{2,1,0:T(8,128)(2,1)}, u32[]{:S(2)}) copy-start(bf16[1,7168,128]{2,1,0:T(8,128)(2,1)} %param.29) | copy-start | bytes 5505028
  394.2 2.5 copy-start.18
  396.8 37.4 %copy-start.4 = (bf16[2048,192]{0,1:T(8,128)(2,1)S(1)}, bf16[2048,192]{0,1:T(8,128)(2,1)}, u32[]{:S(2)}) copy-start(bf16[2048,192]{0,1:T(8,128)(2,1)} %copy.73) | copy-start | bytes 2359300
  434.2 3.8 copy-start.2
  434.2 3.8 copy-start.16
  440.5 32.7 %copy-start.12 = (s32[64,8]{0,1:T(8,128)S(1)}, s32[64,8]{0,1:T(8,128)}, u32[]{:S(2)}) copy-start(s32[64,8]{0,1:T(8,128)} %param.26) | copy-start | bytes 6148
  440.5 32.7 %copy-start.14 = (f32[64,8]{0,1:T(8,128)S(1)}, f32[64,8]{0,1:T(8,128)}, u32[]{:S(2)}) copy-start(f32[64,8]{0,1:T(8,128)} %param.27) | copy-start | bytes 6148
  440.5 44.9 %copy-start.7 = (bf16[64,448]{1,0:T(8,128)(2,1)S(1)}, bf16[64,448]{1,0:T(8,128)(2,1)}, u32[]{:S(2)}) copy-start(bf16[64,448]{1,0:T(8,128)(2,1)} %copy-done.6) | copy-start | bytes 172036
  466.3 19.0 %all-to-all-start.6 = ((bf16[16,40,448]{2,1,0:T(8,128)(2,1)}), bf16[16,40,448]{2,1,0:T(8,128)(2,1)S(1)}, u32[]{:S(2)}, u32[]{:S(2)}) async-start(bf16[16,40,448]{2,1,0:T(8,128)(2,1)} %all_to_all.50), calls=%async_computation.6 | async-start | bytes 1310720 | tf_op jit(solution)/shard_map/all_to_all | solution.py:169
Sparse Core Ops, SparseCore 0:
  53.2 51.1 all-gather.3
  400.1 34.0 all-gather.5
